TPU v7x, 512 devices: a whole 4x4x16 slice. The times are simulated.
512 devices in a mesh: dp: 32 (over y, z_hi, x), tensor: 16 (over z_lo, core).
Axes of the slice: x: 4, y: 4, z: 16 (z_hi: 2, z_lo: 8; z = z_hi * 8 + z_lo), core: 2. Of those that a mesh axis runs over, the one named last changes fastest.
Arguments:
- inner_x: bfloat16 [32768, 8192], P(('dp', 'tensor')), parts along dimension 0, may hold values from -6 to 6
- inner_bc: bfloat16 [32768, 2048], P(('dp', 'tensor')), parts along dimension 0, may hold values from -6 to 6
- step_raw: bfloat16 [32768, 128], P(('dp', 'tensor')), parts along dimension 0, may hold values from -5 to 5
- conv_state_x: bfloat16 [96, 8192], P('dp', 'tensor'), parts along dimension 0, may hold values from -6 to 6
- conv_state_bc: bfloat16 [96, 2048], P('dp'), parts along dimension 0, may hold values from -6 to 6
- conv_weight_x: bfloat16 [4, 8192], P(None, 'tensor'), may hold values from -3 to 3
- conv_bias_x: bfloat16 [8192], P('tensor'), may hold values from -3 to 3
- conv_weight_bc: bfloat16 [4, 2048], replicated, may hold values from -3 to 3
- conv_bias_bc: bfloat16 [2048], replicated, may hold values from -3 to 3
- step_bias: float32 [128], P('tensor'), may hold values from -4 to -2
- decay_rate: float32 [128], P('tensor'), may hold values from 0 to 1, as said below
- skip_gain: float32 [128], P('tensor'), may hold values from 0.5 to 1.5
- norm_weight: bfloat16 [8192], replicated, may hold values from 0.5 to 1.5
- scan_state: float32 [4096, 64, 256], P(('dp', 'tensor')), parts along dimension 0, may hold values from -3 to 3
Outputs:
- normed: bfloat16 [32768, 8192], P(('dp', 'tensor')), parts along dimension 0
- final_state: float32 [4096, 64, 256], P(('dp', 'tensor')), parts along dimension 0
- conv_tail_x: bfloat16 [96, 8192], P('dp', 'tensor'), parts along dimension 0
- conv_tail_bc: bfloat16 [96, 2048], P('dp', 'tensor'), parts along dimension 0
There are 32 independent parts, one for each index of `dp`. A program takes and returns all parts, laid end to end along the dimension named above; an argument that names none is the same for every part. Nothing has to cross between parts.
Inputs may be any that keep to these rules, and one draw needn't show every extreme that they name: decay_rate lies between 2 / 1024 and 1 / 2.
All inputs are finite; a program needn't handle non-finite values.
Results may differ from a plain program's by a relative error of at most 0.0051.
Values may be sent and summed in bfloat16 or wider, within the bound.
No kernel may reach another device: no remote copies, remote signals or barrier semaphores. Data moves between devices by JAX's collectives and lax.ppermute only.
A program may use at most 64 MiB of HBM per device.

v0:
```python
import functools
import jax
import jax.numpy as jnp
from jax import lax
import numpy as np
from jax.sharding import Mesh, PartitionSpec as P

HEAD_DIM = 64
STATE = 256
GROUPS = 4
CONV_K = 4
INNER = 8192
EPSILON = 1e-05
TENSOR = ("tg", "tj")


def causal_conv(raw, state, weight, bias):
    length = raw.shape[0]
    padded = jnp.concatenate([state.astype(jnp.float32), raw.astype(jnp.float32)], axis=0)
    total = jnp.zeros(raw.shape, jnp.float32) + bias.astype(jnp.float32)[None, :]
    for kernel_tap in range(CONV_K):
        total = (
            total
            + weight[kernel_tap].astype(jnp.float32)[None, :]
            * padded[kernel_tap : kernel_tap + length]
        )
    return jax.nn.silu(total).astype(jnp.bfloat16)


def state_mix(
    mixed_x, mixed_bc, step_raw, step_bias, decay_rate, skip_gain, scan_state, groups_here
):
    length = mixed_x.shape[0]
    heads_here = step_raw.shape[1]
    per_group = heads_here // groups_here
    step_size = jax.nn.softplus(step_raw.astype(jnp.float32) + step_bias[None, :])
    running = jnp.cumsum(-step_size * decay_rate[None, :], axis=0)
    halves = mixed_bc.reshape(length, groups_here, 2, STATE)
    input_map = halves[:, :, 0, :]
    output_map = halves[:, :, 1, :]
    step_cols = jnp.transpose(step_size)
    running_cols = jnp.transpose(running)
    query_rows = min(512, length)
    pieces = []
    for row_start in range(0, length, query_rows):
        row_stop = row_start + query_rows
        scores = jnp.einsum(
            "tgn,sgn->gts",
            output_map[row_start:row_stop],
            input_map[:row_stop],
            preferred_element_type=jnp.float32,
        )
        causal = row_start + lax.broadcasted_iota(
            jnp.int32, (query_rows, row_stop), 0
        ) >= lax.broadcasted_iota(jnp.int32, (query_rows, row_stop), 1)
        visible = mixed_x[:row_stop]

        def one_head(
            item,
            scores=scores,
            causal=causal,
            visible=visible,
            row_start=row_start,
            row_stop=row_stop,
        ):
            head_index, step_head, running_head = item
            group_scores = lax.dynamic_index_in_dim(
                scores, head_index // per_group, 0, keepdims=False
            )
            log_gap = running_head[row_start:row_stop, None] - running_head[None, :row_stop]
            decayed = jnp.exp(jnp.where(causal, log_gap, 0.0))
            weights = jnp.where(
                causal, group_scores * decayed * step_head[None, :row_stop], 0.0
            ).astype(jnp.bfloat16)
            values = lax.dynamic_slice_in_dim(visible, head_index * HEAD_DIM, HEAD_DIM, 1)
            return jnp.dot(weights, values, preferred_element_type=jnp.float32)

        local_mix = lax.map(
            one_head, (jnp.arange(heads_here, dtype=jnp.int32), step_cols, running_cols)
        )
        pieces.append(
            jnp.transpose(local_mix, (1, 0, 2)).reshape(query_rows, heads_here * HEAD_DIM)
        )
    local_all = jnp.concatenate(pieces, axis=0)
    grouped_state = scan_state.reshape(groups_here, per_group, HEAD_DIM, STATE)
    carried = jnp.einsum(
        "tgn,ghpn->tghp",
        output_map.astype(jnp.float32),
        grouped_state,
        precision=lax.Precision.HIGHEST,
    )
    carried = carried.reshape(length, heads_here, HEAD_DIM) * jnp.exp(running)[:, :, None]
    channels = mixed_x.reshape(length, heads_here, HEAD_DIM).astype(jnp.float32)
    mixed = (
        local_all.reshape(length, heads_here, HEAD_DIM)
        + carried
        + skip_gain[None, :, None] * channels
    )
    mixed_y = mixed.reshape(length, heads_here * HEAD_DIM).astype(jnp.bfloat16)
    tail_decay = jnp.exp(running[length - 1][None, :] - running) * step_size
    weighted = (
        input_map.astype(jnp.float32)[:, :, None, :]
        * tail_decay.reshape(length, groups_here, per_group)[:, :, :, None]
    ).astype(jnp.bfloat16)
    gathered_in = jnp.einsum(
        "tghp,tghn->ghpn",
        mixed_x.reshape(length, groups_here, per_group, HEAD_DIM),
        weighted,
        preferred_element_type=jnp.float32,
    )
    final = (
        jnp.exp(running[length - 1]).reshape(groups_here, per_group)[:, :, None, None]
        * grouped_state
        + gathered_in
    )
    return (mixed_y, final.reshape(heads_here, HEAD_DIM, STATE))


def group_norm(mixed_y, norm_weight):
    rows = mixed_y.shape[0]
    values = mixed_y.astype(jnp.float32).reshape(rows, GROUPS, INNER // GROUPS)
    mean_square = jnp.mean(values * values, axis=2, keepdims=True)
    scaled = (values * lax.rsqrt(mean_square + EPSILON)).reshape(rows, INNER)
    return (scaled * norm_weight.astype(jnp.float32)[None, :]).astype(jnp.bfloat16)


def local(
    inner_x,
    inner_bc,
    step_raw,
    conv_state_x,
    conv_state_bc,
    conv_weight_x,
    conv_bias_x,
    conv_weight_bc,
    conv_bias_bc,
    step_bias,
    decay_rate,
    skip_gain,
    norm_weight,
    scan_state,
    *,
    group_size,
    tensor_count
):
    device_rank = lax.axis_index("tg") * group_size + lax.axis_index("tj")
    token_rows = inner_x.shape[0]
    heads_here = step_bias.shape[0]
    x_width = heads_here * HEAD_DIM
    bc_width = inner_bc.shape[1] // tensor_count
    x_send = jnp.transpose(inner_x.reshape(token_rows, tensor_count, x_width), (1, 0, 2))
    bc_send = jnp.transpose(inner_bc.reshape(token_rows, tensor_count, bc_width), (1, 0, 2))
    step_send = jnp.transpose(step_raw.reshape(token_rows, tensor_count, heads_here), (1, 0, 2))
    send = jnp.concatenate(
        [
            x_send.reshape(tensor_count, -1),
            bc_send.reshape(tensor_count, -1),
            step_send.reshape(tensor_count, -1),
        ],
        axis=1,
    )
    recv = lax.all_to_all(send, TENSOR, 0, 0, tiled=True)
    length = tensor_count * token_rows
    x_end = token_rows * x_width
    bc_end = x_end + token_rows * bc_width
    head_x = recv[:, :x_end].reshape(length, x_width)
    head_bc_part = recv[:, x_end:bc_end].reshape(length, bc_width)
    head_step = recv[:, bc_end:].reshape(length, heads_here)
    column_start = device_rank * bc_width
    own_state_bc = lax.dynamic_slice_in_dim(conv_state_bc, column_start, bc_width, 1)
    own_weight_bc = lax.dynamic_slice_in_dim(conv_weight_bc, column_start, bc_width, 1)
    own_bias_bc = lax.dynamic_slice_in_dim(conv_bias_bc, column_start, bc_width, 0)
    mixed_bc_part = causal_conv(head_bc_part, own_state_bc, own_weight_bc, own_bias_bc)
    mixed_bc = lax.all_gather(mixed_bc_part, "tj", axis=1, tiled=True)
    mixed_x = causal_conv(head_x, conv_state_x, conv_weight_x, conv_bias_x)
    mixed_y, final_state = state_mix(
        mixed_x, mixed_bc, head_step, step_bias, decay_rate, skip_gain, scan_state, 1
    )
    token_y = lax.all_to_all(mixed_y, TENSOR, split_axis=0, concat_axis=1, tiled=True)
    normed = group_norm(token_y, norm_weight)
    tail_x = head_x[length - CONV_K + 1 :]
    tail_bc = head_bc_part[length - CONV_K + 1 :]
    return (normed, final_state, tail_x, tail_bc)


def solution(mesh):
    dp_count = mesh.shape["dp"]
    tensor_count = mesh.shape["tensor"]
    group_size = tensor_count // GROUPS
    grouped = Mesh(
        np.asarray(mesh.devices).reshape(dp_count, GROUPS, group_size), ("dp", "tg", "tj")
    )
    rows = ("dp",) + TENSOR
    return jax.shard_map(
        functools.partial(local, group_size=group_size, tensor_count=tensor_count),
        mesh=grouped,
        in_specs=(
            P(rows, None),
            P(rows, None),
            P(rows, None),
            P("dp", TENSOR),
            P("dp", None),
            P(None, TENSOR),
            P(TENSOR),
            P(),
            P(),
            P(TENSOR),
            P(TENSOR),
            P(TENSOR),
            P(),
            P(rows, None, None),
        ),
        out_specs=(P(rows, None), P(rows, None, None), P("dp", TENSOR), P("dp", TENSOR)),
        check_vma=False,
    )
```

profile of v0, /device:TPU:65, one launch (start us, length us, event | category | flops | bytes accessed | tf_op | source)
XLA Modules:
  0.0 247.7 jit_solution(4635555850143321165)
XLA Ops:
  7.2 0.9 copy.152
  8.7 0.6 copy.173
  9.4 0.5 broadcast.53
  9.9 1.7 reduce.7
  11.7 1.3 reshape.197
  12.9 12.5 %all-to-all-start = ((bf16[16,2,20736]{2,1,0:T(2,128)(2,1)}), bf16[16,2,20736]{2,1,0:T(2,128)(2,1)}, u32[]{:S(2)}, u32[]{:S(2)}) async-start(bf16[16,2,20736]{2,1,0:T(2,128)(2,1)} %reshape.197), calls=%async_computation | async-start | bytes 2654208 | tf_op jit(solution)/shard_map/all_to_all | solution.py:162
  25.6 0.8 dynamic-slice_convert_fusion.1
  26.4 0.7 constant_dynamic-slice_fusion.4
  27.1 0.7 dynamic-slice_convert_fusion
  27.8 58.0 %all-to-all-done = bf16[16,2,20736]{2,1,0:T(2,128)(2,1)} async-done(((bf16[16,2,20736]{2,1,0:T(2,128)(2,1)}), bf16[16,2,20736]{2,1,0:T(2,128)(2,1)}, u32[]{:S(2)}, u32[]{:S(2)}) %all-to-all-start) | async-done | bytes 1327136 | tf_op jit(solution)/shard_map/all_to_all | solution.py:162
  85.7 4.4 %reshape.198 = bf16[16,1,41472]{2,1,0:T(2,128)(2,1)S(1)} reshape(bf16[16,2,20736]{2,1,0:T(2,128)(2,1)} %all-to-all-done) | data formatting | bytes 2654208
  90.3 1.1 copy-done.5
  91.6 1.1 multiply_convert_fusion.6
  92.8 1.0 slice.147
  93.8 1.6 reshape.178
  96.1 2.3 reduce-window.6
  99.0 1.4 multiply_convert_fusion.3
  101.0 1.8 copy.163
  102.8 15.7 %all-gather.2.cloned.1.call-done = bf16[1024,512]{1,0:T(8,128)(2,1)} async-done(((bf16[1024,128]{1,0:T(8,128)(2,1)}), bf16[1024,512]{1,0:T(8,128)(2,1)}) %all-gather.2.cloned.1.call-update) | async-done | bytes 1048592 | tf_op jit(solution)/shard_map/all_gather | solution.py:174
  118.6 1.5 copy.156
  120.4 1.8 convolution_bitcast_fusion.2
  122.3 13.6 %while.24 = (s32[]{:T(128)}, f32[8,512,64]{1,2,0:T(8,128)S(1)}, f32[1,512,512]{2,1,0:T(8,128)S(1)}, f32[8,1024]{1,0:T(8,128)S(1)}, f32[8,1024]{1,0:T(8,128)S(1)}...) while((s32[]{:T(128)}, f32[8,512,64]{1,2,0:T(8,128)S(1)}, ...), condition=%wide.region_3.4_spmd.clone.clone, body=%wide.region_2.3_spmd.clone.clone.sunk | while | flops 35389444 | bytes 1325243 | solution.py:78
  122.3 0.6 dynamic_slice.73
  124.0 0.6 dynamic_slice.73
  125.7 0.6 dynamic_slice.73
  127.0 0.4 fusion.68
  127.4 0.6 dynamic_slice.73
  129.1 0.6 dynamic_slice.73
  130.8 0.6 dynamic_slice.73
  132.1 0.4 fusion.68
  132.5 0.6 dynamic_slice.73
  134.2 0.6 dynamic_slice.73
  135.5 0.4 fusion.68
  135.9 1.3 copy.159
  137.4 30.9 %while.25 = (s32[]{:T(128)}, f32[8,512,64]{1,2,0:T(8,128)S(1)}, f32[1,512,1024]{2,1,0:T(8,128)}, f32[8,1024]{1,0:T(8,128)S(1)}, f32[8,1024]{1,0:T(8,128)S(1)}, /...) while((s32[]{:T(128)}, f32[8,512,64]{1,2,0:T(8,128)S(1)}, ...), condition=%wide.region_5.6_spmd.clone.clone, body=%wide.region_4.5_spmd.clone.clone.sunk | while | flops 70778888 | bytes 2523355 | solution.py:78
  137.4 0.6 dynamic_slice.76
  138.7 2.5 %fusion.71 = f32[8,512,64]{1,2,0:T(8,128)S(1)} fusion(f32[8,512,64]{1,2,0:T(8,128)S(1)} %get-tuple-element.426, s32[]{:T(128)S(6)} %copy.197, f32[1,512,1024]{2,1,0:T(8,128)} %get-tuple-element.440, s32[512]{0:T(512)S(1)} %get-tuple-element.445, f32[1024]{0:T(1024)S(1)} %bitcast.197, f32[1024]{0:T(1024)S(1)} %bitcast.198, f32[512]{0:T(512)S(1)} %bitcast.201, ...), kind=kOutput, calls=%fused_computation.28.clone.1 | convolution fusion | flops 70778880 | bytes 2502664 | tf_op jit(solution)/shard_map/while/body/eval_jaxpr/dot_general | solution.py:76
  141.3 0.6 dynamic_slice.76
  142.6 2.5 %fusion.71 = f32[8,512,64]{1,2,0:T(8,128)S(1)} fusion(f32[8,512,64]{1,2,0:T(8,128)S(1)} %get-tuple-element.426, s32[]{:T(128)S(6)} %copy.197, f32[1,512,1024]{2,1,0:T(8,128)} %get-tuple-element.440, s32[512]{0:T(512)S(1)} %get-tuple-element.445, f32[1024]{0:T(1024)S(1)} %bitcast.197, f32[1024]{0:T(1024)S(1)} %bitcast.198, f32[512]{0:T(512)S(1)} %bitcast.201, ...), kind=kOutput, calls=%fused_computation.28.clone.1 | convolution fusion | flops 70778880 | bytes 2502664 | tf_op jit(solution)/shard_map/while/body/eval_jaxpr/dot_general | solution.py:76
  145.1 0.6 dynamic_slice.76
  146.5 2.5 %fusion.71 = f32[8,512,64]{1,2,0:T(8,128)S(1)} fusion(f32[8,512,64]{1,2,0:T(8,128)S(1)} %get-tuple-element.426, s32[]{:T(128)S(6)} %copy.197, f32[1,512,1024]{2,1,0:T(8,128)} %get-tuple-element.440, s32[512]{0:T(512)S(1)} %get-tuple-element.445, f32[1024]{0:T(1024)S(1)} %bitcast.197, f32[1024]{0:T(1024)S(1)} %bitcast.198, f32[512]{0:T(512)S(1)} %bitcast.201, ...), kind=kOutput, calls=%fused_computation.28.clone.1 | convolution fusion | flops 70778880 | bytes 2502664 | tf_op jit(solution)/shard_map/while/body/eval_jaxpr/dot_general | solution.py:76
  149.0 0.6 dynamic_slice.76
  150.3 2.5 %fusion.71 = f32[8,512,64]{1,2,0:T(8,128)S(1)} fusion(f32[8,512,64]{1,2,0:T(8,128)S(1)} %get-tuple-element.426, s32[]{:T(128)S(6)} %copy.197, f32[1,512,1024]{2,1,0:T(8,128)} %get-tuple-element.440, s32[512]{0:T(512)S(1)} %get-tuple-element.445, f32[1024]{0:T(1024)S(1)} %bitcast.197, f32[1024]{0:T(1024)S(1)} %bitcast.198, f32[512]{0:T(512)S(1)} %bitcast.201, ...), kind=kOutput, calls=%fused_computation.28.clone.1 | convolution fusion | flops 70778880 | bytes 2502664 | tf_op jit(solution)/shard_map/while/body/eval_jaxpr/dot_general | solution.py:76
  152.9 0.6 dynamic_slice.76
  154.2 2.5 %fusion.71 = f32[8,512,64]{1,2,0:T(8,128)S(1)} fusion(f32[8,512,64]{1,2,0:T(8,128)S(1)} %get-tuple-element.426, s32[]{:T(128)S(6)} %copy.197, f32[1,512,1024]{2,1,0:T(8,128)} %get-tuple-element.440, s32[512]{0:T(512)S(1)} %get-tuple-element.445, f32[1024]{0:T(1024)S(1)} %bitcast.197, f32[1024]{0:T(1024)S(1)} %bitcast.198, f32[512]{0:T(512)S(1)} %bitcast.201, ...), kind=kOutput, calls=%fused_computation.28.clone.1 | convolution fusion | flops 70778880 | bytes 2502664 | tf_op jit(solution)/shard_map/while/body/eval_jaxpr/dot_general | solution.py:76
  156.7 0.6 dynamic_slice.76
  158.1 2.5 %fusion.71 = f32[8,512,64]{1,2,0:T(8,128)S(1)} fusion(f32[8,512,64]{1,2,0:T(8,128)S(1)} %get-tuple-element.426, s32[]{:T(128)S(6)} %copy.197, f32[1,512,1024]{2,1,0:T(8,128)} %get-tuple-element.440, s32[512]{0:T(512)S(1)} %get-tuple-element.445, f32[1024]{0:T(1024)S(1)} %bitcast.197, f32[1024]{0:T(1024)S(1)} %bitcast.198, f32[512]{0:T(512)S(1)} %bitcast.201, ...), kind=kOutput, calls=%fused_computation.28.clone.1 | convolution fusion | flops 70778880 | bytes 2502664 | tf_op jit(solution)/shard_map/while/body/eval_jaxpr/dot_general | solution.py:76
  160.6 0.6 dynamic_slice.76
  161.9 2.5 %fusion.71 = f32[8,512,64]{1,2,0:T(8,128)S(1)} fusion(f32[8,512,64]{1,2,0:T(8,128)S(1)} %get-tuple-element.426, s32[]{:T(128)S(6)} %copy.197, f32[1,512,1024]{2,1,0:T(8,128)} %get-tuple-element.440, s32[512]{0:T(512)S(1)} %get-tuple-element.445, f32[1024]{0:T(1024)S(1)} %bitcast.197, f32[1024]{0:T(1024)S(1)} %bitcast.198, f32[512]{0:T(512)S(1)} %bitcast.201, ...), kind=kOutput, calls=%fused_computation.28.clone.1 | convolution fusion | flops 70778880 | bytes 2502664 | tf_op jit(solution)/shard_map/while/body/eval_jaxpr/dot_general | solution.py:76
  164.5 0.6 dynamic_slice.76
  165.8 2.5 %fusion.71 = f32[8,512,64]{1,2,0:T(8,128)S(1)} fusion(f32[8,512,64]{1,2,0:T(8,128)S(1)} %get-tuple-element.426, s32[]{:T(128)S(6)} %copy.197, f32[1,512,1024]{2,1,0:T(8,128)} %get-tuple-element.440, s32[512]{0:T(512)S(1)} %get-tuple-element.445, f32[1024]{0:T(1024)S(1)} %bitcast.197, f32[1024]{0:T(1024)S(1)} %bitcast.198, f32[512]{0:T(512)S(1)} %bitcast.201, ...), kind=kOutput, calls=%fused_computation.28.clone.1 | convolution fusion | flops 70778880 | bytes 2502664 | tf_op jit(solution)/shard_map/while/body/eval_jaxpr/dot_general | solution.py:76
  168.3 1.3 copy.160
  169.6 2.2 fusion.52
  171.8 1.8 copy.162
  173.7 4.8 %fusion.42 = bf16[1024,512]{1,0:T(8,128)(2,1)} fusion(f32[512,512]{1,0:T(8,128)} %copy.160, f32[512,512]{1,0:T(8,128)} %copy.159, bf16[1024,512]{1,0:T(8,128)(2,1)S(1)} %get-tuple-element.485, f32[1024,512]{1,0:T(8,128)} %copy.162, f32[1024,512]{1,0:T(8,128)} %copy.163, f32[512]{0:T(512)S(1)} %mul.284), kind=kLoop, calls=%fused_computation.55 | loop fusion | flops 3670016 | bytes 8390656 | tf_op jit(solution)/shard_map/convert_element_type | solution.py:99
  178.4 10.2 %all-to-all-start.1 = ((bf16[16,64,512]{2,1,0:T(8,128)(2,1)}), bf16[16,64,512]{2,1,0:T(8,128)(2,1)S(1)}, u32[]{:S(2)}, u32[]{:S(2)}) async-start(bf16[16,64,512]{2,1,0:T(8,128)(2,1)} %bitcast.184), calls=%async_computation.1 | async-start | bytes 2097152 | tf_op jit(solution)/shard_map/all_to_all | solution.py:179
  188.7 1.2 slice.158
  189.9 1.3 slice.157
  191.2 1.3 copy.166
  192.6 1.3 copy.167
  193.9 3.8 %fusion.43 = f32[8,64,256]{2,1,0:T(8,128)} fusion(bf16[1024,8,64]{0,2,1:T(8,128)(2,1)} %bitcast.190, f32[1024,8]{0,1:T(8,128)S(1)} %get-tuple-element.299, f32[1024,256]{1,0:T(8,128)} %copy.167, f32[8,64,256]{2,1,0:T(8,128)S(1)} %copy-done.8, f32[8]{0:T(128)S(1)} %exp.35), kind=kOutput, calls=%fused_computation.62 | convolution fusion | flops 272891904 | bytes 3178528 | tf_op jit(solution)/shard_map/tghp,tghn->ghpn/dot_general | solution.py:105
  197.7 39.6 %all-to-all-done.1 = bf16[16,64,512]{2,1,0:T(8,128)(2,1)S(1)} async-done(((bf16[16,64,512]{2,1,0:T(8,128)(2,1)}), bf16[16,64,512]{2,1,0:T(8,128)(2,1)S(1)}, u32[]{:S(2)}, u32[]{:S(2)}) %all-to-all-start.1) | async-done | bytes 1048608 | tf_op jit(solution)/shard_map/all_to_all | solution.py:179
  238.5 1.2 copy.176
  239.7 1.2 multiply_convert_fusion.2
  (113 shorter events, 8.1 us)
Async XLA Ops:
  7.2 1.2 copy-start
  7.2 1.4 copy-start.10
  11.6 13.8 %copy-start.15 = (bf16[512]{0:T(512)(128)(2,1)S(1)}, bf16[512]{0:T(512)(128)(2,1)}, u32[]{:S(2)}) copy-start(bf16[512]{0:T(512)(128)(2,1)} %param.24) | copy-start | bytes 3076
  11.6 13.8 %copy-start.17 = (f32[8]{0:T(128)S(1)}, f32[8]{0:T(128)}, u32[]{:S(2)}) copy-start(f32[8]{0:T(128)} %param.29) | copy-start | bytes 100
  11.6 14.0 %copy-start.13 = (bf16[3,512]{1,0:T(4,128)(2,1)S(1)}, bf16[3,512]{1,0:T(4,128)(2,1)}, u32[]{:S(2)}) copy-start(bf16[3,512]{1,0:T(4,128)(2,1)} %param.21) | copy-start | bytes 9220
  11.6 16.1 %copy-start.12 = (bf16[4,512]{1,0:T(4,128)(2,1)S(1)}, bf16[4,512]{1,0:T(4,128)(2,1)}, u32[]{:S(2)}) copy-start(bf16[4,512]{1,0:T(4,128)(2,1)} %param.23) | copy-start | bytes 12292
  12.9 72.8 %all-to-all-start = ((bf16[16,2,20736]{2,1,0:T(2,128)(2,1)}), bf16[16,2,20736]{2,1,0:T(2,128)(2,1)}, u32[]{:S(2)}, u32[]{:S(2)}) async-start(bf16[16,2,20736]{2,1,0:T(2,128)(2,1)} %reshape.197), calls=%async_computation | async-start | bytes 2654208 | tf_op jit(solution)/shard_map/all_to_all | solution.py:162
  25.4 93.2 %all-gather.2.cloned.1.call-start = ((), (), s32[]{:S(2)}) async-start(), calls=%async_computation.2 | async-start | bytes 1310720 | tf_op jit(solution)/shard_map/all_gather | solution.py:174
  90.3 1.1 copy-start.5
  91.4 1.4 copy-start.6
  91.5 3.9 %copy-start.9 = (bf16[1024,128]{1,0:T(8,128)(2,1)}, bf16[1024,128]{1,0:T(8,128)(2,1)S(1)}, u32[]{:S(2)}) copy-start(bf16[1024,128]{1,0:T(8,128)(2,1)S(1)} %reshape.172) | copy-start | bytes 786436
  93.8 2.1 copy-start.14
  93.8 2.1 copy-start.16
  95.4 3.6 %copy-start.7 = (bf16[1024,512]{1,0:T(8,128)(2,1)}, bf16[1024,512]{1,0:T(8,128)(2,1)S(1)}, u32[]{:S(2)}) copy-start(bf16[1024,512]{1,0:T(8,128)(2,1)S(1)} %reshape.178) | copy-start | bytes 3145732
  100.4 2.4 copy-start.1
  120.1 2.1 copy-start.3
  120.4 1.9 slice-start
  135.9 1.5 copy-start.2
  178.4 10.2 %copy-start.11 = (bf16[8192]{0:T(1024)(128)(2,1)S(1)}, bf16[8192]{0:T(1024)(128)(2,1)}, u32[]{:S(2)}) copy-start(bf16[8192]{0:T(1024)(128)(2,1)} %param.30) | copy-start | bytes 49156
  178.4 14.0 %copy-start.4 = (bf16[1024,512]{0,1:T(8,128)(2,1)S(1)}, bf16[1024,512]{0,1:T(8,128)(2,1)}, u32[]{:S(2)}) copy-start(bf16[1024,512]{0,1:T(8,128)(2,1)} %copy-done.3) | copy-start | bytes 3145732
  178.4 58.8 %all-to-all-start.1 = ((bf16[16,64,512]{2,1,0:T(8,128)(2,1)}), bf16[16,64,512]{2,1,0:T(8,128)(2,1)S(1)}, u32[]{:S(2)}, u32[]{:S(2)}) async-start(bf16[16,64,512]{2,1,0:T(8,128)(2,1)} %bitcast.184), calls=%async_computation.1 | async-start | bytes 2097152 | tf_op jit(solution)/shard_map/all_to_all | solution.py:179
  192.6 1.3 copy-start.8
Sparse Core Ops, SparseCore 0:
  92.8 25.7 all-gather.1
where the time goes:
time: 249 us; the launch traced here: 248 us
  waiting for transfers between devices  113 us (45%)
  local copies, waits for them, and re-layouts  39.5 us (16%)
  matrix products  31.5 us (13%)
  starting transfers between devices  22.7 us (9%)
  other arithmetic  15.3 us (6%)
  between operations  14.5 us (6%)
  loops' own time  10.8 us (4%)
    all_to_all x1, waiting for transfers between devices, local(): recv = lax.all_to_all(send, TENSOR, 0, 0, tiled=True)  58 us
    all_to_all x1, waiting for transfers between devices, local(): lax.all_to_all(mixed_y, TENSOR, split_axis=0, concat_axis=1, tiled=True)  39.6 us
    dot_general x16, matrix products, one_head(): return jnp.dot(weights, values, preferred_element_type=jnp.float32)  23.5 us
    all_gather x1, waiting for transfers between devices, local(): mixed_bc = lax.all_gather(mixed_bc_part, 'tj', axis=1, tiled=True)  15.7 us
    all_to_all x1, starting transfers between devices, local(): recv = lax.all_to_all(send, TENSOR, 0, 0, tiled=True)  12.5 us
    another operation x2, loops' own time, state_mix(): lax.map(one_head, (jnp.arange(heads_here, dtype=jnp.int32), step_cols, ru...  10.8 us
    all_to_all x1, starting transfers between devices, local(): lax.all_to_all(mixed_y, TENSOR, split_axis=0, concat_axis=1, tiled=True)  10.2 us
    unnamed x44, local copies, waits for them, and re-layouts  9.96 us
  transfers between devices with their start and end apart: 3, of which 3 were waited for; matrix products, arithmetic and copies ran while one was open for 9% of the time, Pallas kernels for 0%

commit v1 on v0

--- a/solution.py
+++ b/solution.py
@@ -4,6 +4,7 @@
 from jax import lax
 import numpy as np
 from jax.sharding import Mesh, PartitionSpec as P
+from jax.lax import all_to_all, axis_size
 
 HEAD_DIM = 64
 STATE = 256
@@ -171,7 +172,9 @@
     own_weight_bc = lax.dynamic_slice_in_dim(conv_weight_bc, column_start, bc_width, 1)
     own_bias_bc = lax.dynamic_slice_in_dim(conv_bias_bc, column_start, bc_width, 0)
     mixed_bc_part = causal_conv(head_bc_part, own_state_bc, own_weight_bc, own_bias_bc)
-    mixed_bc = lax.all_gather(mixed_bc_part, "tj", axis=1, tiled=True)
+    mixed_bc = jnp.concatenate(
+        all_to_all(jnp.stack([mixed_bc_part] * axis_size("tj")), "tj", 0, 0), axis=1
+    )
     mixed_x = causal_conv(head_x, conv_state_x, conv_weight_x, conv_bias_x)
     mixed_y, final_state = state_mix(
         mixed_x, mixed_bc, head_step, step_bias, decay_rate, skip_gain, scan_state, 1

time: 249 us -> 222 us (0.89)
  the two profiles are of different devices: /device:TPU:65 before, /device:TPU:79 now
where the time goes in v1:
time: 222 us; the launch traced here: 221 us
  waiting for transfers between devices  98.2 us (44%)
  local copies, waits for them, and re-layouts  42.4 us (19%)
  matrix products  31.5 us (14%)
  starting transfers between devices  22.8 us (10%)
  other arithmetic  14.6 us (7%)
  loops' own time  10.8 us (5%)
    all_to_all x1, waiting for transfers between devices, local(): recv = lax.all_to_all(send, TENSOR, 0, 0, tiled=True)  58.2 us
    all_to_all x1, waiting for transfers between devices, local(): lax.all_to_all(mixed_y, TENSOR, split_axis=0, concat_axis=1, tiled=True)  39.5 us
    dot_general x16, matrix products, one_head(): return jnp.dot(weights, values, preferred_element_type=jnp.float32)  23.5 us
    all_to_all x1, starting transfers between devices, local(): recv = lax.all_to_all(send, TENSOR, 0, 0, tiled=True)  12.5 us
    another operation x2, loops' own time, state_mix(): lax.map(one_head, (jnp.arange(heads_here, dtype=jnp.int32), step_cols, ru...  10.8 us
    unnamed x44, local copies, waits for them, and re-layouts  9.82 us
    dynamic_slice x24, local copies, waits for them, and re-layouts, state_mix(): lax.map(one_head, (jnp.arange(heads_here, dtype=jnp.int32), step_cols, ru...  9.47 us
    all_to_all x1, starting transfers between devices, local(): lax.all_to_all(mixed_y, TENSOR, split_axis=0, concat_axis=1, tiled=True)  6.8 us
  transfers between devices with their start and end apart: 3, of which 3 were waited for; matrix products, arithmetic and copies ran while one was open for 11% of the time, Pallas kernels for 0%

profile of v1, /device:TPU:79, one launch (start us, length us, event | category | flops | bytes accessed | tf_op | source)
XLA Modules:
  0.0 221.4 jit_solution(4748677072235049546)
XLA Ops:
  0.7 0.9 copy.151
  2.2 0.6 copy.172
  2.9 0.5 broadcast.55
  3.4 1.7 reduce.7
  5.1 1.2 reshape.199
  6.3 12.5 %all-to-all-start = ((bf16[16,2,20736]{2,1,0:T(2,128)(2,1)}), bf16[16,2,20736]{2,1,0:T(2,128)(2,1)}, u32[]{:S(2)}, u32[]{:S(2)}) async-start(bf16[16,2,20736]{2,1,0:T(2,128)(2,1)} %reshape.199), calls=%async_computation | async-start | bytes 2654208 | tf_op jit(solution)/shard_map/all_to_all | solution.py:163
  18.8 0.8 dynamic-slice_convert_fusion.1
  19.5 0.7 constant_dynamic-slice_fusion.4
  20.2 0.7 dynamic-slice_convert_fusion
  20.9 58.2 %all-to-all-done = bf16[16,2,20736]{2,1,0:T(2,128)(2,1)} async-done(((bf16[16,2,20736]{2,1,0:T(2,128)(2,1)}), bf16[16,2,20736]{2,1,0:T(2,128)(2,1)}, u32[]{:S(2)}, u32[]{:S(2)}) %all-to-all-start) | async-done | bytes 1327136 | tf_op jit(solution)/shard_map/all_to_all | solution.py:163
  79.1 4.4 %reshape.200 = bf16[16,1,41472]{2,1,0:T(2,128)(2,1)S(1)} reshape(bf16[16,2,20736]{2,1,0:T(2,128)(2,1)} %all-to-all-done) | data formatting | bytes 2654208
  83.7 1.1 copy-done.5
  85.5 1.1 stack.2
  86.6 3.5 %all-to-all-start.1 = ((bf16[4,1024,128]{1,2,0:T(8,128)(2,1)}), bf16[4,1024,128]{1,2,0:T(8,128)(2,1)S(1)}, u32[]{:S(2)}, u32[]{:S(2)}) async-start(bf16[4,1024,128]{1,2,0:T(8,128)(2,1)} %stack.2), calls=%async_computation.1 | async-start | bytes 2097152 | tf_op jit(solution)/shard_map/all_to_all | solution.py:176
  90.4 1.0 slice.147
  91.4 2.4 %reshape.180 = bf16[1024,512]{1,0:T(8,128)(2,1)} reshape(bf16[16,32768]{1,0:T(8,128)(2,1)} %slice.147) | data formatting | bytes 2097152 | tf_op jit(solution)/shard_map/reshape | solution.py:167
  94.4 2.3 %reduce-window.6 = f32[8,8,128]{2,1,0:T(8,128)S(1)} reduce-window(f32[8,8,128]{2,1,0:T(8,128)S(1)} %copy.157, f32[]{:T(128)} %constant.83.clone.1), window={size=1x1x128 pad=0_0x0_0x127_0}, to_apply=%region_0.1 | reduce-window | flops 1040384 | bytes 65540 | tf_op jit(solution)/shard_map/reduce-window
  97.4 1.4 multiply_convert_fusion.3
  99.1 1.6 mul.280
  100.7 2.9 %copy.162 = f32[1024,512]{1,0:T(8,128)} copy(f32[1024,512]{0,1:T(8,128)} %bitcast.181) | data formatting | bytes 4194304 | tf_op jit(solution)/shard_map/mul | solution.py:93
  103.6 0.4 all-to-all-done.1
  104.4 1.8 convolution_bitcast_fusion.2
  106.3 13.6 %while.24 = (s32[]{:T(128)}, f32[8,512,64]{1,2,0:T(8,128)S(1)}, f32[1,512,512]{2,1,0:T(8,128)S(1)}, f32[8,1024]{1,0:T(8,128)S(1)}, f32[8,1024]{1,0:T(8,128)S(1)}...) while((s32[]{:T(128)}, f32[8,512,64]{1,2,0:T(8,128)S(1)}, ...), condition=%wide.region_3.4_spmd.clone.clone, body=%wide.region_2.3_spmd.clone.clone.sunk | while | flops 35389444 | bytes 1325243 | solution.py:79
  106.3 0.6 dynamic_slice.73
  108.0 0.6 dynamic_slice.73
  109.7 0.6 dynamic_slice.73
  111.4 0.6 dynamic_slice.73
  113.1 0.6 dynamic_slice.73
  114.8 0.6 dynamic_slice.73
  116.0 0.4 fusion.68
  116.5 0.6 dynamic_slice.73
  118.2 0.6 dynamic_slice.73
  119.4 0.4 fusion.68
  119.9 1.4 copy.158
  121.3 30.9 %while.25 = (s32[]{:T(128)}, f32[8,512,64]{1,2,0:T(8,128)S(1)}, f32[1,512,1024]{2,1,0:T(8,128)}, f32[8,1024]{1,0:T(8,128)S(1)}, f32[8,1024]{1,0:T(8,128)S(1)}, /...) while((s32[]{:T(128)}, f32[8,512,64]{1,2,0:T(8,128)S(1)}, ...), condition=%wide.region_5.6_spmd.clone.clone, body=%wide.region_4.5_spmd.clone.clone.sunk | while | flops 70778888 | bytes 2523355 | solution.py:79
  121.4 0.6 dynamic_slice.76
  122.7 2.5 %fusion.71 = f32[8,512,64]{1,2,0:T(8,128)S(1)} fusion(f32[8,512,64]{1,2,0:T(8,128)S(1)} %get-tuple-element.426, s32[]{:T(128)S(6)} %copy.196, f32[1,512,1024]{2,1,0:T(8,128)} %get-tuple-element.440, s32[512]{0:T(512)S(1)} %get-tuple-element.445, f32[1024]{0:T(1024)S(1)} %bitcast.199, f32[1024]{0:T(1024)S(1)} %bitcast.200, f32[512]{0:T(512)S(1)} %bitcast.203, ...), kind=kOutput, calls=%fused_computation.28.clone.1 | convolution fusion | flops 70778880 | bytes 2502664 | tf_op jit(solution)/shard_map/while/body/eval_jaxpr/dot_general | solution.py:77
  125.2 0.6 dynamic_slice.76
  126.6 2.5 %fusion.71 = f32[8,512,64]{1,2,0:T(8,128)S(1)} fusion(f32[8,512,64]{1,2,0:T(8,128)S(1)} %get-tuple-element.426, s32[]{:T(128)S(6)} %copy.196, f32[1,512,1024]{2,1,0:T(8,128)} %get-tuple-element.440, s32[512]{0:T(512)S(1)} %get-tuple-element.445, f32[1024]{0:T(1024)S(1)} %bitcast.199, f32[1024]{0:T(1024)S(1)} %bitcast.200, f32[512]{0:T(512)S(1)} %bitcast.203, ...), kind=kOutput, calls=%fused_computation.28.clone.1 | convolution fusion | flops 70778880 | bytes 2502664 | tf_op jit(solution)/shard_map/while/body/eval_jaxpr/dot_general | solution.py:77
  129.1 0.6 dynamic_slice.76
  130.4 2.5 %fusion.71 = f32[8,512,64]{1,2,0:T(8,128)S(1)} fusion(f32[8,512,64]{1,2,0:T(8,128)S(1)} %get-tuple-element.426, s32[]{:T(128)S(6)} %copy.196, f32[1,512,1024]{2,1,0:T(8,128)} %get-tuple-element.440, s32[512]{0:T(512)S(1)} %get-tuple-element.445, f32[1024]{0:T(1024)S(1)} %bitcast.199, f32[1024]{0:T(1024)S(1)} %bitcast.200, f32[512]{0:T(512)S(1)} %bitcast.203, ...), kind=kOutput, calls=%fused_computation.28.clone.1 | convolution fusion | flops 70778880 | bytes 2502664 | tf_op jit(solution)/shard_map/while/body/eval_jaxpr/dot_general | solution.py:77
  132.9 0.6 dynamic_slice.76
  134.3 2.5 %fusion.71 = f32[8,512,64]{1,2,0:T(8,128)S(1)} fusion(f32[8,512,64]{1,2,0:T(8,128)S(1)} %get-tuple-element.426, s32[]{:T(128)S(6)} %copy.196, f32[1,512,1024]{2,1,0:T(8,128)} %get-tuple-element.440, s32[512]{0:T(512)S(1)} %get-tuple-element.445, f32[1024]{0:T(1024)S(1)} %bitcast.199, f32[1024]{0:T(1024)S(1)} %bitcast.200, f32[512]{0:T(512)S(1)} %bitcast.203, ...), kind=kOutput, calls=%fused_computation.28.clone.1 | convolution fusion | flops 70778880 | bytes 2502664 | tf_op jit(solution)/shard_map/while/body/eval_jaxpr/dot_general | solution.py:77
  136.8 0.6 dynamic_slice.76
  138.2 2.5 %fusion.71 = f32[8,512,64]{1,2,0:T(8,128)S(1)} fusion(f32[8,512,64]{1,2,0:T(8,128)S(1)} %get-tuple-element.426, s32[]{:T(128)S(6)} %copy.196, f32[1,512,1024]{2,1,0:T(8,128)} %get-tuple-element.440, s32[512]{0:T(512)S(1)} %get-tuple-element.445, f32[1024]{0:T(1024)S(1)} %bitcast.199, f32[1024]{0:T(1024)S(1)} %bitcast.200, f32[512]{0:T(512)S(1)} %bitcast.203, ...), kind=kOutput, calls=%fused_computation.28.clone.1 | convolution fusion | flops 70778880 | bytes 2502664 | tf_op jit(solution)/shard_map/while/body/eval_jaxpr/dot_general | solution.py:77
  140.7 0.6 dynamic_slice.76
  142.0 2.5 %fusion.71 = f32[8,512,64]{1,2,0:T(8,128)S(1)} fusion(f32[8,512,64]{1,2,0:T(8,128)S(1)} %get-tuple-element.426, s32[]{:T(128)S(6)} %copy.196, f32[1,512,1024]{2,1,0:T(8,128)} %get-tuple-element.440, s32[512]{0:T(512)S(1)} %get-tuple-element.445, f32[1024]{0:T(1024)S(1)} %bitcast.199, f32[1024]{0:T(1024)S(1)} %bitcast.200, f32[512]{0:T(512)S(1)} %bitcast.203, ...), kind=kOutput, calls=%fused_computation.28.clone.1 | convolution fusion | flops 70778880 | bytes 2502664 | tf_op jit(solution)/shard_map/while/body/eval_jaxpr/dot_general | solution.py:77
  144.6 0.6 dynamic_slice.76
  145.9 2.5 %fusion.71 = f32[8,512,64]{1,2,0:T(8,128)S(1)} fusion(f32[8,512,64]{1,2,0:T(8,128)S(1)} %get-tuple-element.426, s32[]{:T(128)S(6)} %copy.196, f32[1,512,1024]{2,1,0:T(8,128)} %get-tuple-element.440, s32[512]{0:T(512)S(1)} %get-tuple-element.445, f32[1024]{0:T(1024)S(1)} %bitcast.199, f32[1024]{0:T(1024)S(1)} %bitcast.200, f32[512]{0:T(512)S(1)} %bitcast.203, ...), kind=kOutput, calls=%fused_computation.28.clone.1 | convolution fusion | flops 70778880 | bytes 2502664 | tf_op jit(solution)/shard_map/while/body/eval_jaxpr/dot_general | solution.py:77
  148.4 0.6 dynamic_slice.76
  149.8 2.5 %fusion.71 = f32[8,512,64]{1,2,0:T(8,128)S(1)} fusion(f32[8,512,64]{1,2,0:T(8,128)S(1)} %get-tuple-element.426, s32[]{:T(128)S(6)} %copy.196, f32[1,512,1024]{2,1,0:T(8,128)} %get-tuple-element.440, s32[512]{0:T(512)S(1)} %get-tuple-element.445, f32[1024]{0:T(1024)S(1)} %bitcast.199, f32[1024]{0:T(1024)S(1)} %bitcast.200, f32[512]{0:T(512)S(1)} %bitcast.203, ...), kind=kOutput, calls=%fused_computation.28.clone.1 | convolution fusion | flops 70778880 | bytes 2502664 | tf_op jit(solution)/shard_map/while/body/eval_jaxpr/dot_general | solution.py:77
  152.3 1.3 copy.159
  153.6 2.2 fusion.52
  155.8 1.8 copy.161
  157.6 4.7 %fusion.42 = bf16[1024,512]{1,0:T(8,128)(2,1)} fusion(f32[512,512]{1,0:T(8,128)} %copy.159, f32[512,512]{1,0:T(8,128)} %copy.158, bf16[1024,512]{1,0:T(8,128)(2,1)S(1)} %get-tuple-element.484, f32[1024,512]{1,0:T(8,128)} %copy.161, f32[1024,512]{1,0:T(8,128)} %copy.162, f32[512]{0:T(512)S(1)} %mul.284), kind=kLoop, calls=%fused_computation.55 | loop fusion | flops 3670016 | bytes 8390656 | tf_op jit(solution)/shard_map/convert_element_type | solution.py:100
  162.4 6.8 %all-to-all-start.2 = ((bf16[16,64,512]{2,1,0:T(8,128)(2,1)}), bf16[16,64,512]{2,1,0:T(8,128)(2,1)S(1)}, u32[]{:S(2)}, u32[]{:S(2)}) async-start(bf16[16,64,512]{2,1,0:T(8,128)(2,1)} %bitcast.186), calls=%async_computation.2 | async-start | bytes 2097152 | tf_op jit(solution)/shard_map/all_to_all | solution.py:182
  169.2 1.3 slice.158
  170.4 1.3 slice.157
  171.7 1.3 copy.165
  173.2 1.3 copy.166
  174.5 3.8 %fusion.43 = f32[8,64,256]{2,1,0:T(8,128)} fusion(bf16[1024,8,64]{0,2,1:T(8,128)(2,1)} %bitcast.192, f32[1024,8]{0,1:T(8,128)S(1)} %get-tuple-element.299, f32[1024,256]{1,0:T(8,128)} %copy.166, f32[8,64,256]{2,1,0:T(8,128)S(1)} %copy-done.8, f32[8]{0:T(128)S(1)} %exp.35), kind=kOutput, calls=%fused_computation.62 | convolution fusion | flops 272891904 | bytes 3178528 | tf_op jit(solution)/shard_map/tghp,tghn->ghpn/dot_general | solution.py:106
  178.2 39.5 %all-to-all-done.2 = bf16[16,64,512]{2,1,0:T(8,128)(2,1)S(1)} async-done(((bf16[16,64,512]{2,1,0:T(8,128)(2,1)}), bf16[16,64,512]{2,1,0:T(8,128)(2,1)S(1)}, u32[]{:S(2)}, u32[]{:S(2)}) %all-to-all-start.2) | async-done | bytes 1048608 | tf_op jit(solution)/shard_map/all_to_all | solution.py:182
  219.0 1.2 copy.175
  220.2 1.2 multiply_convert_fusion.2
  (113 shorter events, 8.5 us)
Async XLA Ops:
  0.6 1.2 copy-start
  0.6 1.4 copy-start.10
  6.3 72.8 %all-to-all-start = ((bf16[16,2,20736]{2,1,0:T(2,128)(2,1)}), bf16[16,2,20736]{2,1,0:T(2,128)(2,1)}, u32[]{:S(2)}, u32[]{:S(2)}) async-start(bf16[16,2,20736]{2,1,0:T(2,128)(2,1)} %reshape.199), calls=%async_computation | async-start | bytes 2654208 | tf_op jit(solution)/shard_map/all_to_all | solution.py:163
  83.7 1.1 copy-start.5
  84.9 1.7 copy-start.9
  85.3 4.8 %copy-start.15 = (bf16[512]{0:T(512)(128)(2,1)S(1)}, bf16[512]{0:T(512)(128)(2,1)}, u32[]{:S(2)}) copy-start(bf16[512]{0:T(512)(128)(2,1)} %param.24) | copy-start | bytes 3076
  85.3 4.8 %copy-start.17 = (f32[8]{0:T(128)S(1)}, f32[8]{0:T(128)}, u32[]{:S(2)}) copy-start(f32[8]{0:T(128)} %param.29) | copy-start | bytes 100
  85.4 5.0 %copy-start.13 = (bf16[3,512]{1,0:T(4,128)(2,1)S(1)}, bf16[3,512]{1,0:T(4,128)(2,1)}, u32[]{:S(2)}) copy-start(bf16[3,512]{1,0:T(4,128)(2,1)} %param.21) | copy-start | bytes 9220
  85.4 5.0 %copy-start.12 = (bf16[4,512]{1,0:T(4,128)(2,1)S(1)}, bf16[4,512]{1,0:T(4,128)(2,1)}, u32[]{:S(2)}) copy-start(bf16[4,512]{1,0:T(4,128)(2,1)} %param.23) | copy-start | bytes 12292
  85.4 5.0 %copy-start.6 = (bf16[16,1,41472]{2,0,1:T(8,128)(2,1)S(1)}, bf16[16,1,41472]{2,0,1:T(8,128)(2,1)}, u32[]{:S(2)}) copy-start(bf16[16,1,41472]{2,0,1:T(8,128)(2,1)} %copy-done.5) | copy-start | bytes 3981316
  86.6 17.4 %all-to-all-start.1 = ((bf16[4,1024,128]{1,2,0:T(8,128)(2,1)}), bf16[4,1024,128]{1,2,0:T(8,128)(2,1)S(1)}, u32[]{:S(2)}, u32[]{:S(2)}) async-start(bf16[4,1024,128]{1,2,0:T(8,128)(2,1)} %stack.2), calls=%async_computation.1 | async-start | bytes 2097152 | tf_op jit(solution)/shard_map/all_to_all | solution.py:176
  91.4 2.9 %copy-start.14 = (f32[8]{0:T(128)S(1)}, f32[8]{0:T(128)}, u32[]{:S(2)}) copy-start(f32[8]{0:T(128)} %param.27) | copy-start | bytes 100
  91.4 2.9 %copy-start.16 = (f32[8]{0:T(128)S(1)}, f32[8]{0:T(128)}, u32[]{:S(2)}) copy-start(f32[8]{0:T(128)} %param.28) | copy-start | bytes 100
  93.8 3.3 %copy-start.7 = (bf16[1024,512]{1,0:T(8,128)(2,1)S(1)}, bf16[1024,512]{1,0:T(8,128)(2,1)}, u32[]{:S(2)}) copy-start(bf16[1024,512]{1,0:T(8,128)(2,1)} %reshape.180) | copy-start | bytes 3145732
  98.8 4.8 %copy-start.1 = (bf16[1024,512]{1,0:T(8,128)(2,1)}, bf16[1024,512]{1,0:T(8,128)(2,1)S(1)}, u32[]{:S(2)}) copy-start(bf16[1024,512]{1,0:T(8,128)(2,1)S(1)} %multiply_convert_fusion.3) | copy-start | bytes 3145732
  104.0 2.1 copy-start.3
  104.3 1.9 slice-start
  119.8 1.5 copy-start.2
  162.4 6.8 %copy-start.11 = (bf16[8192]{0:T(1024)(128)(2,1)S(1)}, bf16[8192]{0:T(1024)(128)(2,1)}, u32[]{:S(2)}) copy-start(bf16[8192]{0:T(1024)(128)(2,1)} %param.30) | copy-start | bytes 49156
  162.4 10.7 %copy-start.4 = (bf16[4,1024,128]{1,2,0:T(8,128)(2,1)S(1)}, bf16[4,1024,128]{1,2,0:T(8,128)(2,1)}, u32[]{:S(2)}) copy-start(bf16[4,1024,128]{1,2,0:T(8,128)(2,1)} %copy-done.3) | copy-start | bytes 3145732
  162.4 55.4 %all-to-all-start.2 = ((bf16[16,64,512]{2,1,0:T(8,128)(2,1)}), bf16[16,64,512]{2,1,0:T(8,128)(2,1)S(1)}, u32[]{:S(2)}, u32[]{:S(2)}) async-start(bf16[16,64,512]{2,1,0:T(8,128)(2,1)} %bitcast.186), calls=%async_computation.2 | async-start | bytes 2097152 | tf_op jit(solution)/shard_map/all_to_all | solution.py:182
  173.2 1.3 copy-start.8
